TPU v7x, 256 devices: a whole 4x4x8 slice. The times are simulated.
256 devices in a mesh: row: 16 (over z, core), col: 16 (over x, y).
Axes of the slice: x: 4, y: 4, z: 8, core: 2. Of those that a mesh axis runs over, the one named last changes fastest.
Arguments:
- site_tensor: bfloat16 [1024, 4, 1024], P('row', None, 'col'), may hold values from -180 to 180
- site_tangent: bfloat16 [1024, 4, 1024], P('row', None, 'col'), may hold values from -180 to 180
- left_env: bfloat16 [1024, 16384], P('row', 'col'), may hold values from -0.1875 to 0.375
- right_env: bfloat16 [1024, 16384], P('row', 'col'), may hold values from -0.046875 to 0.09375
- mpo: bfloat16 [16, 16, 4, 4], replicated, may hold values from -0.25 to 0.75
- dissipation: float32 [4], replicated, may hold values from 0.2 to 2
Outputs:
- evolved: float32 [1024, 4, 1024], P('row', None, 'col')
- evolved_tangent: float32 [1024, 4, 1024], P('row', None, 'col')
All inputs are finite; a program needn't handle non-finite values.
Results may differ from a plain program's by a relative error of at most 0.0055.
Values may be sent and summed in bfloat16 or wider, within the bound.
No kernel may reach another device: no remote copies, remote signals or barrier semaphores. Data moves between devices by JAX's collectives and lax.ppermute only.
A program may use at most 64 MiB of HBM per device.

v0:
```python
import jax
import jax.numpy as jnp
from jax import lax
from jax.sharding import PartitionSpec as P

KRYLOV = 3
taylor_order = 16


def inner(first, second):
    return jnp.sum(first * second)


def total(values):
    return lax.psum(lax.psum(values, "col"), "row")


def taylor(hess, dhess):
    size = hess.shape[0]
    term = jnp.zeros((size,), jnp.float32).at[0].set(1.0)
    dterm = jnp.zeros((size,), jnp.float32)
    total = term
    dtotal = dterm
    for order in range(1, taylor_order + 1):
        nterm = jnp.dot(hess, term, precision=lax.Precision.HIGHEST) / order
        dterm = (
            jnp.dot(dhess, term, precision=lax.Precision.HIGHEST)
            + jnp.dot(hess, dterm, precision=lax.Precision.HIGHEST)
        ) / order
        term = nterm
        total = total + term
        dtotal = dtotal + dterm
    return (total, dtotal)


def local(site_tensor, site_tangent, left_env, right_env, mpo, dissipation):
    rows_here, physical, cols_here = site_tensor.shape
    channels = mpo.shape[0]
    left_whole = lax.all_gather(left_env, "col", axis=1, tiled=True)
    right_whole = lax.all_gather(right_env, "row", axis=0, tiled=True)

    def apply(stacked):
        panels = stacked.shape[1]
        whole = lax.all_gather(stacked.astype(jnp.bfloat16), "row", axis=0, tiled=True)
        flat = whole.reshape(whole.shape[0], panels * physical * cols_here)
        left_three = left_whole.reshape(rows_here, flat.shape[0], channels)
        mixed = lax.dot_general(
            left_three, flat, (((1,), (0,)), ((), ())), preferred_element_type=jnp.float32
        )
        mixed = mixed.astype(jnp.bfloat16).reshape(rows_here, channels, panels, physical, cols_here)
        channel = jnp.einsum("awspr,wvpq->asqrv", mixed, mpo, preferred_element_type=jnp.float32)
        channel = channel.astype(jnp.bfloat16).reshape(
            rows_here * panels * physical, cols_here * channels
        )
        partial_rows = lax.dot_general(
            channel, right_whole, (((1,), (1,)), ((), ())), preferred_element_type=jnp.float32
        )
        partial_rows = partial_rows.reshape(rows_here, panels, physical, partial_rows.shape[1])
        summed = lax.psum_scatter(partial_rows, "col", scatter_dimension=3, tiled=True)
        return summed - dissipation[None, None, :, None] * stacked

    primal = site_tensor.astype(jnp.float32)
    tangent = site_tangent.astype(jnp.float32)
    starting = total(jnp.stack([inner(primal, primal), inner(primal, tangent)]))
    norm_site = jnp.sqrt(starting[0])
    norm_tangent = starting[1] / norm_site
    basis = [primal / norm_site]
    tangents = [(tangent - basis[0] * norm_tangent) / norm_site]
    hess = jnp.zeros((KRYLOV, KRYLOV), jnp.float32)
    dhess = jnp.zeros((KRYLOV, KRYLOV), jnp.float32)
    gram = jnp.zeros((KRYLOV, KRYLOV), jnp.float32)
    cross = jnp.zeros((KRYLOV, KRYLOV), jnp.float32)
    for level in range(KRYLOV):
        both = apply(jnp.stack([basis[level], tangents[level]], axis=1))
        image = both[:, 0]
        dimage = both[:, 1]
        counted = level + 1
        locals_list = [inner(vector, image) for vector in basis]
        locals_list = locals_list + [inner(vector, image) for vector in tangents]
        locals_list = locals_list + [inner(vector, dimage) for vector in basis]
        last = level + 1 == KRYLOV
        if not last:
            newest = basis[level]
            locals_list = locals_list + [inner(image, image), inner(image, dimage)]
            locals_list = locals_list + [inner(newest, vector) for vector in basis]
            locals_list = locals_list + [inner(newest, vector) for vector in tangents]
            locals_list = locals_list + [inner(vector, tangents[level]) for vector in basis[:level]]
        totals = total(jnp.stack(locals_list))
        coeffs = totals[:counted]
        across = totals[counted : 2 * counted]
        along = totals[2 * counted : 3 * counted]
        dcoeffs = across + along
        hess = hess.at[:counted, level].set(coeffs)
        dhess = dhess.at[:counted, level].set(dcoeffs)
        if not last:
            at = 3 * counted
            squared_image = totals[at]
            image_dimage = totals[at + 1]
            at += 2
            gram = gram.at[level, :counted].set(totals[at : at + counted])
            gram = gram.at[:counted, level].set(totals[at : at + counted])
            at += counted
            cross = cross.at[level, :counted].set(totals[at : at + counted])
            at += counted
            cross = cross.at[:level, level].set(totals[at : at + level])
            g = gram[:counted, :counted]
            t = cross[:counted, :counted]
            squared = (
                squared_image
                - 2.0 * jnp.sum(coeffs * coeffs)
                + jnp.dot(
                    coeffs,
                    jnp.dot(g, coeffs, precision=lax.Precision.HIGHEST),
                    precision=lax.Precision.HIGHEST,
                )
            )
            mixed_term = (
                image_dimage
                - jnp.sum(dcoeffs * coeffs)
                - jnp.sum(coeffs * across)
                - jnp.sum(coeffs * along)
                + jnp.dot(
                    coeffs,
                    jnp.dot(g, dcoeffs, precision=lax.Precision.HIGHEST),
                    precision=lax.Precision.HIGHEST,
                )
                + jnp.dot(
                    coeffs,
                    jnp.dot(t, coeffs, precision=lax.Precision.HIGHEST),
                    precision=lax.Precision.HIGHEST,
                )
            )
            residual = image
            dresidual = dimage
            for index in range(counted):
                residual = residual - coeffs[index] * basis[index]
                dresidual = (
                    dresidual - dcoeffs[index] * basis[index] - coeffs[index] * tangents[index]
                )
            height = jnp.sqrt(squared)
            dheight = mixed_term / height
            newvec = residual / height
            basis.append(newvec)
            tangents.append((dresidual - newvec * dheight) / height)
            hess = hess.at[level + 1, level].set(height)
            dhess = dhess.at[level + 1, level].set(dheight)
    coeff, dcoeff = taylor(hess, dhess)
    spread = jnp.zeros_like(primal)
    dspread = jnp.zeros_like(primal)
    for index in range(KRYLOV):
        spread = spread + coeff[index] * basis[index]
        dspread = dspread + coeff[index] * tangents[index] + dcoeff[index] * basis[index]
    evolved = norm_site * spread
    evolved_tangent = norm_tangent * spread + norm_site * dspread
    return (evolved, evolved_tangent)


def solution(mesh):
    in_specs = (
        P("row", None, "col"),
        P("row", None, "col"),
        P("row", "col"),
        P("row", "col"),
        P(),
        P(),
    )
    out_specs = (P("row", None, "col"), P("row", None, "col"))
    return jax.shard_map(local, mesh=mesh, in_specs=in_specs, out_specs=out_specs, check_vma=False)
```

profile of v0, /device:TPU:1, one launch (start us, length us, event | category | flops | bytes accessed | tf_op | source)
XLA Modules:
  0.0 870.2 jit_solution(10881828648179970118)
XLA Ops:
  10.1 34.2 %psum.56 = f32[2]{0:T(128)S(1)} all-reduce(f32[2]{0:T(128)S(1)} %pad_maximum_fusion.3), channel_id=1, replica_groups=mesh['row'=16,'col'=16] {'col'}, use_global_device_ids=true, to_apply=%region_2.0 | all-reduce | flops 2 | bytes 16 | tf_op jit(solution)/shard_map/psum | solution.py:15
  44.3 33.8 %psum.57 = f32[2]{0:T(128)S(1)} all-reduce(f32[2]{0:T(128)S(1)} %psum.56), channel_id=1, replica_groups=mesh['row'=16,'col'=16] {'row'}, use_global_device_ids=true, to_apply=%region_3.0 | all-reduce | flops 2 | bytes 16 | tf_op jit(solution)/shard_map/psum | solution.py:15
  84.3 32.3 %all-gather.6.cloned.1.call-done = bf16[1024,2,4,64]{3,2,1,0:T(4,128)(2,1)} async-done(((bf16[64,2,4,64]{3,2,1,0:T(4,128)(2,1)}), bf16[1024,2,4,64]{3,2,1,0:T(4,128)(2,1)}) %all-gather.6.cloned.1.call-update) | async-done | bytes 1048592 | tf_op jit(solution)/shard_map/all_gather | solution.py:44
  116.6 4.1 copy.109
  120.7 44.7 %all-gather.8.cloned.1.call-done = bf16[64,16384]{1,0:T(8,128)(2,1)} async-done(((bf16[64,1024]{1,0:T(8,128)(2,1)}), bf16[64,16384]{1,0:T(8,128)(2,1)}) %all-gather.8.cloned.1.call-update) | async-done | bytes 2097168 | tf_op jit(solution)/shard_map/all_gather | solution.py:39
  165.5 4.8 copy.110
  170.2 4.5 copy.112
  174.7 3.5 fusion.18
  178.2 4.7 reshape.536
  182.9 4.7 fusion.9
  187.6 5.8 copy.115
  193.4 14.8 %all-gather.10.cloned.1.call-done = bf16[1024,1024]{1,0:T(8,128)(2,1)} async-done(((bf16[64,1024]{1,0:T(8,128)(2,1)}), bf16[1024,1024]{1,0:T(8,128)(2,1)}) %all-gather.10.cloned.1.call-update) | async-done | bytes 2097168 | tf_op jit(solution)/shard_map/all_gather | solution.py:40
  208.1 6.0 fusion.5
  214.1 4.8 copy.173
  218.9 5.6 reshape.685
  225.0 76.2 %reduce-scatter.10.cloned.1.call-done = f32[64,512]{1,0:T(8,128)} async-done(((f32[1024,512]{1,0:T(8,128)}), f32[64,512]{1,0:T(8,128)}) %reduce-scatter.10.cloned.1.call-update) | async-done | bytes 131088
  303.4 4.5 stack.145
  307.8 30.9 %psum.58 = f32[7]{0:T(128)S(1)} all-reduce(f32[7]{0:T(128)S(1)} %stack.145), channel_id=1, replica_groups=mesh['row'=16,'col'=16] {'col'}, use_global_device_ids=true, to_apply=%region_12.0 | all-reduce | flops 7 | bytes 56 | tf_op jit(solution)/shard_map/psum | solution.py:15
  338.7 32.9 %psum.59 = f32[7]{0:T(128)S(1)} all-reduce(f32[7]{0:T(128)S(1)} %psum.58), channel_id=1, replica_groups=mesh['row'=16,'col'=16] {'row'}, use_global_device_ids=true, to_apply=%region_13.0 | all-reduce | flops 7 | bytes 56 | tf_op jit(solution)/shard_map/psum | solution.py:15
  384.9 35.9 %all-gather.12.cloned.1.call-done = bf16[1024,2,4,64]{3,2,1,0:T(4,128)(2,1)} async-done(((bf16[64,2,4,64]{3,2,1,0:T(4,128)(2,1)}), bf16[1024,2,4,64]{3,2,1,0:T(4,128)(2,1)}) %all-gather.12.cloned.1.call-update) | async-done | bytes 1048592 | tf_op jit(solution)/shard_map/all_gather | solution.py:44
  420.8 4.1 copy.118
  424.9 3.5 fusion.19
  428.4 4.7 reshape.543
  433.1 4.7 fusion.12
  437.7 5.8 copy.123
  443.5 6.0 fusion.3
  449.5 4.8 copy.175
  454.3 5.6 reshape.687
  462.4 74.2 %reduce-scatter.12.cloned.1.call-done = f32[64,512]{1,0:T(8,128)} async-done(((f32[1024,512]{1,0:T(8,128)}), f32[64,512]{1,0:T(8,128)}) %reduce-scatter.12.cloned.1.call-update) | async-done | bytes 131088
  538.8 8.2 stack.162
  547.7 30.9 %psum.60 = f32[13]{0:T(128)S(1)} all-reduce(f32[13]{0:T(128)S(1)} %stack.162), channel_id=1, replica_groups=mesh['row'=16,'col'=16] {'col'}, use_global_device_ids=true, to_apply=%region_28.0 | all-reduce | flops 13 | bytes 104 | tf_op jit(solution)/shard_map/psum | solution.py:15
  578.6 33.1 %psum.61 = f32[13]{0:T(128)S(1)} all-reduce(f32[13]{0:T(128)S(1)} %psum.60), channel_id=1, replica_groups=mesh['row'=16,'col'=16] {'row'}, use_global_device_ids=true, to_apply=%region_29.0 | all-reduce | flops 13 | bytes 104 | tf_op jit(solution)/shard_map/psum | solution.py:15
  617.0 1.8 dynamic-slice.126
  628.2 2.7 subtract_divide_fusion
  631.7 35.9 %all-gather.14.cloned.1.call-done = bf16[1024,2,4,64]{3,2,1,0:T(4,128)(2,1)} async-done(((bf16[64,2,4,64]{3,2,1,0:T(4,128)(2,1)}), bf16[1024,2,4,64]{3,2,1,0:T(4,128)(2,1)}) %all-gather.14.cloned.1.call-update) | async-done | bytes 1048592 | tf_op jit(solution)/shard_map/all_gather | solution.py:44
  667.6 4.1 copy.127
  671.7 3.5 fusion.20
  675.2 3.5 reshape.554
  678.8 3.1 fusion.15
  681.8 5.8 copy.132
  687.6 4.6 fusion.1
  692.3 3.2 copy.177
  695.5 5.6 reshape.689
  704.9 73.0 %reduce-scatter.14.cloned.1.call-done = f32[64,512]{1,0:T(8,128)} async-done(((f32[1024,512]{1,0:T(8,128)}), f32[64,512]{1,0:T(8,128)}) %reduce-scatter.14.cloned.1.call-update) | async-done | bytes 131088
  780.0 5.7 stack.175
  785.9 30.9 %psum.62 = f32[9]{0:T(128)S(1)} all-reduce(f32[9]{0:T(128)S(1)} %stack.175), channel_id=1, replica_groups=mesh['row'=16,'col'=16] {'col'}, use_global_device_ids=true, to_apply=%region_45.0 | all-reduce | flops 9 | bytes 72 | tf_op jit(solution)/shard_map/psum | solution.py:15
  816.9 32.9 %psum.63 = f32[9]{0:T(128)S(1)} all-reduce(f32[9]{0:T(128)S(1)} %psum.62), channel_id=1, replica_groups=mesh['row'=16,'col'=16] {'row'}, use_global_device_ids=true, to_apply=%region_46.0 | all-reduce | flops 9 | bytes 72 | tf_op jit(solution)/shard_map/psum | solution.py:15
  857.8 3.9 multiply_add_fusion
  (130 shorter events, 41.6 us)
Async XLA Ops:
  7.2 109.4 %all-gather.6.cloned.1.call-start = ((), (), s32[]{:S(2)}) async-start(), calls=%async_computation.3 | async-start | bytes 2228224 | tf_op jit(solution)/shard_map/all_gather | solution.py:44
  81.8 83.7 %all-gather.8.cloned.1.call-start = ((), (), s32[]{:S(2)}) async-start(), calls=%async_computation.4 | async-start | bytes 2228224 | tf_op jit(solution)/shard_map/all_gather | solution.py:39
  82.5 125.6 %all-gather.10.cloned.1.call-start = ((), (), s32[]{:S(2)}) async-start(), calls=%async_computation.5 | async-start | bytes 2228224 | tf_op jit(solution)/shard_map/all_gather | solution.py:40
  83.3 218.0 %reduce-scatter.10.cloned.1.call-start = ((), (), s32[]{:S(2)}) async-start(), calls=%async_computation.8 | async-start | bytes 2228224
  224.5 78.0 %copy-start.2 = (f32[4]{0:T(128)S(1)}, f32[4]{0:T(128)}, u32[]{:S(2)}) copy-start(f32[4]{0:T(128)} %param.47) | copy-start | bytes 52
  224.5 78.1 %copy-start = (bf16[64,4,64]{2,1,0:T(4,128)(2,1)S(1)}, bf16[64,4,64]{2,1,0:T(4,128)(2,1)}, u32[]{:S(2)}) copy-start(bf16[64,4,64]{2,1,0:T(4,128)(2,1)} %param.42) | copy-start | bytes 98308
  224.5 78.1 %copy-start.1 = (bf16[64,4,64]{2,1,0:T(4,128)(2,1)S(1)}, bf16[64,4,64]{2,1,0:T(4,128)(2,1)}, u32[]{:S(2)}) copy-start(bf16[64,4,64]{2,1,0:T(4,128)(2,1)} %param.43) | copy-start | bytes 98308
  224.5 196.3 %all-gather.12.cloned.1.call-start = ((), (), s32[]{:S(2)}) async-start(), calls=%async_computation.6 | async-start | bytes 2228224 | tf_op jit(solution)/shard_map/all_gather | solution.py:44
  384.8 151.8 %reduce-scatter.12.cloned.1.call-start = ((), (), s32[]{:S(2)}) async-start(), calls=%async_computation.9 | async-start | bytes 2228224
  459.9 207.7 %all-gather.14.cloned.1.call-start = ((), (), s32[]{:S(2)}) async-start(), calls=%async_computation.7 | async-start | bytes 2228224 | tf_op jit(solution)/shard_map/all_gather | solution.py:44
  631.7 146.2 %reduce-scatter.14.cloned.1.call-start = ((), (), s32[]{:S(2)}) async-start(), calls=%async_computation.10 | async-start | bytes 2228224
  701.1 148.9 %copy-start.3 = (f32[3,1]{0,1:T(1,128)S(1)}, f32[3,1]{0,1:T(1,128)}, u32[]{:S(2)}) copy-start(f32[3,1]{0,1:T(1,128)} %constant.468) | copy-start | bytes 40
Sparse Core Ops, SparseCore 0:
  81.9 34.6 all-gather.5
  119.1 46.3 all-gather.7
  167.3 40.7 all-gather.9
  224.6 76.5 reduce-scatter.9
  385.0 35.7 all-gather.11
  460.0 76.5 reduce-scatter.11
  631.8 35.7 all-gather.13
  701.2 76.6 reduce-scatter.13
where the time goes:
time: 881 us; the launch traced here: 870 us
  waiting for transfers between devices  388 us (44%)
  blocking collectives  260 us (30%)
  local copies, waits for them, and re-layouts  123 us (14%)
  matrix products  48.2 us (5%)
  between operations  34.5 us (4%)
  other arithmetic  15.4 us (2%)
    psum x8, blocking collectives, total(): return lax.psum(lax.psum(values, 'col'), 'row')  260 us
    unnamed x11, waiting for transfers between devices  225 us
    all_gather x3, waiting for transfers between devices, apply(): lax.all_gather(stacked.astype(jnp.bfloat16), 'row', axis=0, tiled=True)  104 us
    all_gather x1, waiting for transfers between devices, local(): left_whole = lax.all_gather(left_env, 'col', axis=1, tiled=True)  44.7 us
    unnamed x23, local copies, waits for them, and re-layouts  35.7 us
    another operation x3, local copies, waits for them, and re-layouts, local(): totals = total(jnp.stack(locals_list))  18.4 us
  transfers between devices with their start and end apart: 8, of which 8 were waited for; matrix products, arithmetic and copies ran while one was open for 5% of the time, Pallas kernels for 0%

commit v1 on v0

--- a/solution.py
+++ b/solution.py
@@ -5,6 +5,29 @@
 
 KRYLOV = 3
 taylor_order = 16
+
+
+def _trace_records(message):
+    arr_out = lax.psum(1, "col")
+    mixed_arr = lax.axis_index("col")
+    answer, row_out, part_next = (arr_out, mixed_arr, message.shape[1])
+    y = tuple((jj * answer if s == 1 else jj for s, jj in enumerate(message.shape)))
+    main = jnp.zeros(y, message.dtype)
+    after = built = message
+    met_up = lax.dynamic_update_slice_in_dim(main, message, row_out * part_next, axis=1)
+    for j in tuple(range(1, answer // 2 + 1)):
+        oldest = tuple(((s, (s + 1) % answer) for s in range(answer)))
+        after = lax.ppermute(after, "col", oldest)
+        met_up = lax.dynamic_update_slice_in_dim(
+            met_up, after, (row_out - j) % answer * part_next, axis=1
+        )
+        if 2 * j < answer:
+            front = tuple(((s, (s - 1) % answer) for s in range(answer)))
+            built = lax.ppermute(built, "col", front)
+            met_up = lax.dynamic_update_slice_in_dim(
+                met_up, built, (row_out + j) % answer * part_next, axis=1
+            )
+    return met_up
 
 
 def inner(first, second):
@@ -36,7 +59,7 @@
 def local(site_tensor, site_tangent, left_env, right_env, mpo, dissipation):
     rows_here, physical, cols_here = site_tensor.shape
     channels = mpo.shape[0]
-    left_whole = lax.all_gather(left_env, "col", axis=1, tiled=True)
+    left_whole = _trace_records(left_env)
     right_whole = lax.all_gather(right_env, "row", axis=0, tiled=True)
 
     def apply(stacked):

time: 881 us -> 848 us (0.963)
  waiting for transfers between devices: 388 us -> 313 us
  starting transfers between devices: 0.79 us -> 35.5 us
  local copies, waits for them, and re-layouts: 123 us -> 135 us
    all_gather x1 -> x0, waiting for transfers between devices: 44.7 us -> none  [local(): left_whole = lax.all_gather(left_env, 'col', axis=1, tiled=True)]
    ppermute x0 -> x15, starting transfers between devices: none -> 34.9 us  [the longest x7 33.8 us: _trace_records(): built = lax.ppermute(built, 'col', front)]
    all_gather x3, waiting for transfers between devices: 104 us -> 71.4 us  [apply(): lax.all_gather(stacked.astype(jnp.bfloat16), 'row', axis=0, tiled=True)]
    all_gather x1, waiting for transfers between devices: 14.8 us -> 0.01 us  [local(): right_whole = lax.all_gather(right_env, 'row', axis=0, tiled=True)]
    dynamic_update_slice x0 -> x16, local copies, waits for them, and re-layouts: none -> 11.7 us  [the longest x8 5.87 us: _trace_records(): lax.dynamic_update_slice_in_dim(met_up, after, (row_out - j) % answer * p...]
    ppermute x0 -> x15, waiting for transfers between devices: none -> 10.5 us  [the longest x8 10.5 us: _trace_records(): after = lax.ppermute(after, 'col', oldest)]
    unnamed x11 -> x10, waiting for transfers between devices: 225 us -> 232 us
    unnamed x23 -> x30, local copies, waits for them, and re-layouts: 35.7 us -> 36.6 us
  transfers between devices with their start and end apart: 8 -> 22, of which waited for: 8 -> 12; matrix products, arithmetic and copies ran while one was open for 5% -> 6% of each run, Pallas kernels for 0% -> 0%
where the time goes in v1:
time: 848 us; the launch traced here: 837 us
  waiting for transfers between devices  313 us (37%)
  blocking collectives  259 us (31%)
  local copies, waits for them, and re-layouts  135 us (16%)
  matrix products  42.7 us (5%)
  between operations  35.8 us (4%)
  starting transfers between devices  35.5 us (4%)
  other arithmetic  15.4 us (2%)
    psum x8, blocking collectives, total(): return lax.psum(lax.psum(values, 'col'), 'row')  259 us
    unnamed x10, waiting for transfers between devices  232 us
    all_gather x3, waiting for transfers between devices, apply(): lax.all_gather(stacked.astype(jnp.bfloat16), 'row', axis=0, tiled=True)  71.4 us
    unnamed x30, local copies, waits for them, and re-layouts  36.6 us
    ppermute x7, starting transfers between devices, _trace_records(): built = lax.ppermute(built, 'col', front)  33.8 us
    another operation x3, local copies, waits for them, and re-layouts, local(): totals = total(jnp.stack(locals_list))  18.3 us
    convert_element_type x3, local copies, waits for them, and re-layouts, apply(): channel.astype(jnp.bfloat16)  17.4 us
  transfers between devices with their start and end apart: 22, of which 12 were waited for; matrix products, arithmetic and copies ran while one was open for 6% of the time, Pallas kernels for 0%

profile of v1, /device:TPU:1, one launch (start us, length us, event | category | flops | bytes accessed | tf_op | source)
XLA Modules:
  0.0 837.0 jit_solution(18180790587305785814)
XLA Ops:
  10.1 34.2 %psum.56 = f32[2]{0:T(128)S(1)} all-reduce(f32[2]{0:T(128)S(1)} %pad_maximum_fusion.3), channel_id=1, replica_groups=mesh['row'=16,'col'=16] {'col'}, use_global_device_ids=true, to_apply=%region_2.3 | all-reduce | flops 2 | bytes 16 | tf_op jit(solution)/shard_map/psum | solution.py:38
  44.3 33.8 %psum.57 = f32[2]{0:T(128)S(1)} all-reduce(f32[2]{0:T(128)S(1)} %psum.56), channel_id=1, replica_groups=mesh['row'=16,'col'=16] {'row'}, use_global_device_ids=true, to_apply=%region_3.4 | all-reduce | flops 2 | bytes 16 | tf_op jit(solution)/shard_map/psum | solution.py:38
  82.7 4.8 collective-permute-start.1
  93.5 4.8 collective-permute-start.3
  101.4 4.9 collective-permute-start.5
  108.8 4.9 collective-permute-start.7
  116.2 4.8 collective-permute-start.9
  123.6 4.8 collective-permute-start.11
  131.3 4.8 collective-permute-start.13
  139.4 6.1 collective-permute-done.14
  146.4 5.8 copy.171
  152.3 2.9 copy.170
  157.5 4.7 reshape.536
  162.2 3.6 fusion.9
  165.9 5.8 copy.175
  171.7 6.0 fusion.5
  177.6 4.8 copy.233
  182.4 5.6 reshape.685
  188.1 82.4 %reduce-scatter.10.cloned.1.call-done = f32[64,512]{1,0:T(8,128)} async-done(((f32[1024,512]{1,0:T(8,128)}), f32[64,512]{1,0:T(8,128)}) %reduce-scatter.10.cloned.1.call-update) | async-done | bytes 131088
  272.7 4.5 stack.145
  277.1 30.9 %psum.58 = f32[7]{0:T(128)S(1)} all-reduce(f32[7]{0:T(128)S(1)} %stack.145), channel_id=1, replica_groups=mesh['row'=16,'col'=16] {'col'}, use_global_device_ids=true, to_apply=%region_12.13 | all-reduce | flops 7 | bytes 56 | tf_op jit(solution)/shard_map/psum | solution.py:38
  308.0 32.9 %psum.59 = f32[7]{0:T(128)S(1)} all-reduce(f32[7]{0:T(128)S(1)} %psum.58), channel_id=1, replica_groups=mesh['row'=16,'col'=16] {'row'}, use_global_device_ids=true, to_apply=%region_13.14 | all-reduce | flops 7 | bytes 56 | tf_op jit(solution)/shard_map/psum | solution.py:38
  355.2 35.7 %all-gather.9.cloned.1.call-done = bf16[1024,2,4,64]{3,2,1,0:T(4,128)(2,1)} async-done(((bf16[64,2,4,64]{3,2,1,0:T(4,128)(2,1)}), bf16[1024,2,4,64]{3,2,1,0:T(4,128)(2,1)}) %all-gather.9.cloned.1.call-update) | async-done | bytes 1048592 | tf_op jit(solution)/shard_map/all_gather | solution.py:67
  390.9 2.9 copy.178
  396.1 4.7 reshape.543
  400.9 3.6 fusion.12
  404.5 5.8 copy.183
  410.3 6.0 fusion.3
  416.3 4.8 copy.235
  421.0 5.6 reshape.687
  429.4 74.0 %reduce-scatter.12.cloned.1.call-done = f32[64,512]{1,0:T(8,128)} async-done(((f32[1024,512]{1,0:T(8,128)}), f32[64,512]{1,0:T(8,128)}) %reduce-scatter.12.cloned.1.call-update) | async-done | bytes 131088
  505.5 8.2 stack.162
  514.4 30.9 %psum.60 = f32[13]{0:T(128)S(1)} all-reduce(f32[13]{0:T(128)S(1)} %stack.162), channel_id=1, replica_groups=mesh['row'=16,'col'=16] {'col'}, use_global_device_ids=true, to_apply=%region_28.29 | all-reduce | flops 13 | bytes 104 | tf_op jit(solution)/shard_map/psum | solution.py:38
  545.3 32.9 %psum.61 = f32[13]{0:T(128)S(1)} all-reduce(f32[13]{0:T(128)S(1)} %psum.60), channel_id=1, replica_groups=mesh['row'=16,'col'=16] {'row'}, use_global_device_ids=true, to_apply=%region_29.30 | all-reduce | flops 13 | bytes 104 | tf_op jit(solution)/shard_map/psum | solution.py:38
  594.8 2.7 subtract_divide_fusion
  598.5 35.7 %all-gather.11.cloned.1.call-done = bf16[1024,2,4,64]{3,2,1,0:T(4,128)(2,1)} async-done(((bf16[64,2,4,64]{3,2,1,0:T(4,128)(2,1)}), bf16[1024,2,4,64]{3,2,1,0:T(4,128)(2,1)}) %all-gather.11.cloned.1.call-update) | async-done | bytes 1048592 | tf_op jit(solution)/shard_map/all_gather | solution.py:67
  634.2 4.1 copy.187
  638.3 3.5 convolution_convert_fusion
  641.8 3.5 reshape.554
  647.4 5.8 copy.192
  653.2 4.6 fusion.1
  657.8 3.2 copy.237
  661.0 5.6 reshape.689
  669.0 74.3 %reduce-scatter.14.cloned.1.call-done = f32[64,512]{1,0:T(8,128)} async-done(((f32[1024,512]{1,0:T(8,128)}), f32[64,512]{1,0:T(8,128)}) %reduce-scatter.14.cloned.1.call-update) | async-done | bytes 131088
  745.4 5.7 stack.175
  752.4 30.9 %psum.62 = f32[9]{0:T(128)S(1)} all-reduce(f32[9]{0:T(128)S(1)} %stack.175), channel_id=1, replica_groups=mesh['row'=16,'col'=16] {'col'}, use_global_device_ids=true, to_apply=%region_45.46 | all-reduce | flops 9 | bytes 72 | tf_op jit(solution)/shard_map/psum | solution.py:38
  783.4 32.9 %psum.63 = f32[9]{0:T(128)S(1)} all-reduce(f32[9]{0:T(128)S(1)} %psum.62), channel_id=1, replica_groups=mesh['row'=16,'col'=16] {'row'}, use_global_device_ids=true, to_apply=%region_46.47 | all-reduce | flops 9 | bytes 72 | tf_op jit(solution)/shard_map/psum | solution.py:38
  824.3 3.9 multiply_add_fusion
  (195 shorter events, 71.8 us)
Async XLA Ops:
  7.2 145.1 %all-gather.5.cloned.1.call-start = ((), (), s32[]{:S(2)}) async-start(), calls=%async_computation.3 | async-start | bytes 2228224 | tf_op jit(solution)/shard_map/all_gather | solution.py:67
  81.8 89.9 %all-gather.7.cloned.1.call-start = ((), (), s32[]{:S(2)}) async-start(), calls=%async_computation.4 | async-start | bytes 2228224 | tf_op jit(solution)/shard_map/all_gather | solution.py:63
  82.5 188.0 %reduce-scatter.10.cloned.1.call-start = ((), (), s32[]{:S(2)}) async-start(), calls=%async_computation.7 | async-start | bytes 2228224
  82.6 9.7 %collective-permute-start = (bf16[64,1024]{1,0:T(8,128)(2,1)}, bf16[64,1024]{1,0:T(8,128)(2,1)S(1)}, u32[]{:S(2)}, u32[]{:S(2)}) collective-permute-start(bf16[64,1024]{1,0:T(8,128)(2,1)} %param.44), channel_id=1, source_target_pairs={{0,1},{1,2},{2,3},{3,4},{4,5},{5,6},{6,7},{7,8},{8,9},{9,10},{10,1... | collective-permute-start | bytes 393224 | tf_op jit(solution)/shard_map/ppermute | solution.py:20
  82.7 10.6 %collective-permute-start.1 = (bf16[64,1024]{1,0:T(8,128)(2,1)}, bf16[64,1024]{1,0:T(8,128)(2,1)S(1)}, u32[]{:S(2)}, u32[]{:S(2)}) collective-permute-start(bf16[64,1024]{1,0:T(8,128)(2,1)} %param.44), channel_id=1, source_target_pairs={{0,15},{1,0},{2,1},{3,2},{4,3},{5,4},{6,5},{7,6},{8,7},{9,8},{10,9... | collective-permute-start | bytes 393224 | tf_op jit(solution)/shard_map/ppermute | solution.py:26
  88.6 2.9 copy-start.2
  92.5 7.8 collective-permute-start.2
  93.5 7.7 collective-permute-start.3
  100.4 7.2 collective-permute-start.4
  101.4 7.2 collective-permute-start.5
  107.8 7.2 collective-permute-start.6
  108.8 7.2 collective-permute-start.7
  115.2 7.2 collective-permute-start.8
  116.2 7.2 collective-permute-start.9
  122.6 7.2 collective-permute-start.10
  123.6 7.5 collective-permute-start.11
  129.9 7.6 collective-permute-start.12
  131.3 7.2 collective-permute-start.13
  137.7 7.8 collective-permute-start.14
  157.5 4.7 copy-start.3
  188.0 83.7 %copy-start.5 = (f32[4]{0:T(128)S(1)}, f32[4]{0:T(128)}, u32[]{:S(2)}) copy-start(f32[4]{0:T(128)} %param.47) | copy-start | bytes 52
  188.0 83.8 %copy-start = (bf16[64,4,64]{2,1,0:T(4,128)(2,1)S(1)}, bf16[64,4,64]{2,1,0:T(4,128)(2,1)}, u32[]{:S(2)}) copy-start(bf16[64,4,64]{2,1,0:T(4,128)(2,1)} %param.42) | copy-start | bytes 98308
  188.0 83.8 %copy-start.1 = (bf16[64,4,64]{2,1,0:T(4,128)(2,1)S(1)}, bf16[64,4,64]{2,1,0:T(4,128)(2,1)}, u32[]{:S(2)}) copy-start(bf16[64,4,64]{2,1,0:T(4,128)(2,1)} %param.43) | copy-start | bytes 98308
  188.1 202.9 %all-gather.9.cloned.1.call-start = ((), (), s32[]{:S(2)}) async-start(), calls=%async_computation.5 | async-start | bytes 2228224 | tf_op jit(solution)/shard_map/all_gather | solution.py:67
  355.0 148.3 %reduce-scatter.12.cloned.1.call-start = ((), (), s32[]{:S(2)}) async-start(), calls=%async_computation.8 | async-start | bytes 2228224
  396.1 4.7 copy-start.4
  426.7 207.5 %all-gather.11.cloned.1.call-start = ((), (), s32[]{:S(2)}) async-start(), calls=%async_computation.6 | async-start | bytes 2228224 | tf_op jit(solution)/shard_map/all_gather | solution.py:67
  598.3 145.1 %reduce-scatter.14.cloned.1.call-start = ((), (), s32[]{:S(2)}) async-start(), calls=%async_computation.9 | async-start | bytes 2228224
  666.6 150.0 %copy-start.6 = (f32[3,1]{0,1:T(1,128)S(1)}, f32[3,1]{0,1:T(1,128)}, u32[]{:S(2)}) copy-start(f32[3,1]{0,1:T(1,128)} %constant.576) | copy-start | bytes 40
Sparse Core Ops, SparseCore 0:
  81.9 34.6 all-gather.4
  118.4 37.8 all-gather.6
  188.2 82.2 reduce-scatter.9
  355.1 35.7 all-gather.8
  426.8 76.4 reduce-scatter.11
  598.4 35.7 all-gather.10
  666.8 76.5 reduce-scatter.13
